TPU v7x, 512 devices: a whole 4x8x8 slice. The times are simulated.
512 devices in a mesh: ta: 32 (over y, x), pb: 16 (over z, core).
Axes of the slice: x: 4, y: 8, z: 8, core: 2. Of those that a mesh axis runs over, the one named last changes fastest.
Arguments:
- particles: float32 [2, 2097152], P(None, ('ta', 'pb')), may hold values from -6 to 6
- weights: bfloat16 [2097152], P(('ta', 'pb')), may hold values from 0.5 to 2
- cell_index: int32 [2097152], P(('ta', 'pb')), may hold values from 0 to 9215
- target_group: int32 [2097152, 1], P(('ta', 'pb')), may hold values from 0 to 31; in each aligned block of 4096 rows (0 to 4095, 4096 to 8191, ...) at most 256 rows name the same one
- target_slice: int32 [2097152], P(('ta', 'pb')), may hold values from 0 to 3
- laser_x: float32 [96], replicated, may hold values from 0.3 to 1.5
- laser_y: float32 [96], replicated, may hold values from 0.3 to 1.5
- mode_x: float32 [96], replicated, may hold values from 0.3 to 1.5
- mode_y: float32 [96], replicated, may hold values from 0.3 to 1.5
- along_coeff: float32 [96, 96], replicated, may hold values from 0.2 to 2
- across_coeff: float32 [96, 96], replicated, may hold values from 0.1 to 1
Outputs:
- arrivals: float32 [2, 4194304], P(None, ('ta', 'pb'))
- radiation: float32 [2, 128], P(None, 'ta')
Inputs may be any that keep to these rules, and one draw needn't show every extreme that they name: `target_group`: in the rows of one device at most 256 rows name the same group, and in every draw some group is named by exactly 256 rows of some device.
All inputs are finite; a program needn't handle non-finite values.
Results may differ from a plain program's by a relative error of at most 0.0009.
Values sent between devices are 32-bit elements; how exact they have to be, the bound alone decides.
No kernel may reach another device: no remote copies, remote signals or barrier semaphores. Data moves between devices by JAX's collectives and lax.ppermute only.
A program may use at most 64 MiB of HBM per device.

v0:
```python
import math
import jax
import jax.numpy as jnp
from jax import lax
from jax.sharding import PartitionSpec as P

SL_DEV = 4
PS_DEV = 1024
HARM = 48
PERIODS = 2
DISPERSION = 3.0
LASER_GAIN = 1.0
KICK_GAIN = 0.5
SLIP_GAIN = 0.05


def with_halo(x, sides, width):
    for axis, dim in sides:
        peers, length = (lax.axis_size(axis), x.shape[dim])
        up = [(i, (i + 1) % peers) for i in range(peers - 1)]
        down = [(j, i) for i, j in up]
        last = lax.slice_in_dim(x, length - width, length, axis=dim)
        leading = lax.slice_in_dim(x, 0, width, axis=dim)
        before = lax.ppermute(last, axis, up)
        after = lax.ppermute(leading, axis, down)
        x = jnp.concatenate([before, x, after], axis=dim)
    return x


def shifted(value, axis, steps):
    count = lax.axis_size(axis)
    leading, last = (max(0, -steps), min(count, count - steps))
    return lax.ppermute(value, axis, [(source, source + steps) for source in range(leading, last)])


def lookup(values_table, positions):
    matches = positions[None, :] == jnp.arange(values_table.shape[0], dtype=jnp.int32)[:, None]
    return jnp.sum(jnp.where(matches, values_table[:, None], 0.0), axis=0)


def arrival_slots(destination, groups):
    count = destination.shape[0]
    block_size = math.gcd(count, 512)
    turn_count = count // block_size
    onehot = (destination[:, None] == jnp.arange(groups, dtype=jnp.int32)[None, :]).astype(
        jnp.bfloat16
    )
    onehot = onehot.reshape(turn_count, block_size, groups)
    earlier = (jnp.arange(block_size)[:, None] > jnp.arange(block_size)[None, :]).astype(
        jnp.bfloat16
    )

    def count_step(counted, onehot_rows):
        before = (
            jnp.dot(earlier, onehot_rows, preferred_element_type=jnp.float32) + counted[None, :]
        )
        rows_f = onehot_rows.astype(jnp.float32)
        return (counted + jnp.sum(rows_f, axis=0), jnp.sum(before * rows_f, axis=1))

    _, arrival = lax.scan(count_step, jnp.zeros((groups,), jnp.float32), onehot)
    return arrival.reshape(count).astype(jnp.int32)


def deposit(arrived_weight, got_slice, got_cell, slice_count, grid_x, grid_y):
    slot_count = arrived_weight.shape[0]
    block_size = math.gcd(slot_count, 2048)
    turn_count = slot_count // block_size
    block_items = (
        arrived_weight.reshape(turn_count, block_size),
        got_slice.reshape(turn_count, block_size),
        got_cell.reshape(turn_count, block_size),
    )

    def deposit_step(running, items):
        block_weight, block_slice, block_cell = items
        on_slice = block_slice[None, :] == jnp.arange(slice_count, dtype=jnp.int32)[:, None]
        on_row = (block_cell // grid_y)[None, :] == jnp.arange(grid_x, dtype=jnp.int32)[:, None]
        left = jnp.where(
            on_slice[:, None, :] & on_row[None, :, :],
            block_weight[None, None, :],
            jnp.zeros((), jnp.bfloat16),
        )
        left = left.reshape(slice_count * grid_x, block_size)
        right = (
            (block_cell % grid_y)[:, None] == jnp.arange(grid_y, dtype=jnp.int32)[None, :]
        ).astype(jnp.bfloat16)
        return (running + jnp.dot(left, right, preferred_element_type=jnp.float32), None)

    running, _ = lax.scan(
        deposit_step, jnp.zeros((slice_count * grid_x, grid_y), jnp.float32), block_items
    )
    return running.reshape(slice_count, grid_x * grid_y)


def stencil(extended, sideways, coeff_long, coeff_cross, grid_y):
    centre = sideways[:, grid_y:-grid_y]
    along_diff = extended[2:] - extended[:-2]
    across = sideways[:, 2 * grid_y :] + sideways[:, : -2 * grid_y]
    column = jnp.arange(centre.shape[1], dtype=jnp.int32) % grid_y
    upper_y = jnp.where(column < grid_y - 1, jnp.pad(centre, ((0, 0), (0, 1)))[:, 1:], 0.0)
    lower_y = jnp.where(column > 0, jnp.pad(centre, ((0, 0), (1, 0)))[:, :-1], 0.0)
    return coeff_long[None, :] * along_diff + coeff_cross[None, :] * (
        4.0 * centre - across - upper_y - lower_y
    )


def body(
    particles,
    weights,
    cell_index,
    target_group,
    target_slice,
    laser_x,
    laser_y,
    mode_x,
    mode_y,
    along_coeff,
    across_coeff,
):
    groups = lax.axis_size("ta")
    splits = lax.axis_size("pb")
    grid_x = laser_x.shape[0]
    grid_y = laser_y.shape[0]
    cell_count = grid_x * grid_y
    per_device = particles.shape[1]
    capacity = 2 * per_device // groups
    slot_count = groups * capacity
    row_x = cell_index // grid_y
    row_y = cell_index % grid_y
    energy = particles[1] + LASER_GAIN * lookup(laser_x, row_x) * lookup(laser_y, row_y) * jnp.sin(
        particles[0]
    )
    phases = particles[0] + DISPERSION * energy
    destination = target_group[:, 0]
    position = destination * capacity + arrival_slots(destination, groups)
    send_float = (
        jnp.zeros((3, slot_count), jnp.float32)
        .at[:, position]
        .set(jnp.stack([phases, energy, weights.astype(jnp.float32)]))
    )
    send_index = (
        jnp.zeros((1, slot_count), jnp.int32)
        .at[0, position]
        .set(target_slice * cell_count + cell_index)
    )
    got_float, got_index = (
        lax.all_to_all(
            send_float.reshape(3, groups, capacity), "ta", split_axis=1, concat_axis=1, tiled=True
        ),
        lax.all_to_all(
            send_index.reshape(1, groups, capacity), "ta", split_axis=1, concat_axis=1, tiled=True
        ),
    )
    got_float = got_float.reshape(3, slot_count)
    combined = got_index.reshape(slot_count)
    arrived_weight = got_float[2]
    got_slice = combined // cell_count
    got_cell = combined % cell_count
    partial_value = deposit(
        arrived_weight.astype(jnp.bfloat16), got_slice, got_cell, SL_DEV, grid_x, grid_y
    )
    long_flat = along_coeff.reshape(cell_count)
    cross_flat = across_coeff.reshape(cell_count)
    summed = lax.psum(partial_value, "pb")
    extended = with_halo(summed, (("ta", 0),), 1)
    sideways = jnp.pad(extended[1:-1], ((0, 0), (grid_y, grid_y)))
    force_map = stencil(extended, sideways, long_flat, cross_flat, grid_y)
    kicked = got_float[1] + jnp.take(force_map.reshape(-1), combined)
    got_phase = got_float[0]
    profile = lookup(mode_x, got_cell // grid_y) * lookup(mode_y, got_cell % grid_y)
    weighted = arrived_weight * profile
    select = (got_slice[None, :] == jnp.arange(SL_DEV, dtype=jnp.int32)[:, None]).astype(
        jnp.float32
    )
    couple = 1.0 / math.sqrt(splits * PS_DEV)
    radiation = jnp.zeros((2, SL_DEV), jnp.float32)
    for period in range(PERIODS):
        harmonic_phase = HARM * got_phase
        cosine = jnp.cos(harmonic_phase)
        sine_part = jnp.sin(harmonic_phase)
        local_sums = jnp.stack(
            [
                jnp.sum(select * (weighted * cosine)[None, :], axis=1),
                jnp.sum(select * (-weighted * sine_part)[None, :], axis=1),
            ]
        )
        bunching = lax.psum(local_sums, "pb")
        radiation = radiation + couple * bunching
        real_here = jnp.sum(select * radiation[0][:, None], axis=0)
        imag_here = jnp.sum(select * radiation[1][:, None], axis=0)
        kicked = kicked + KICK_GAIN * profile * (real_here * cosine - imag_here * sine_part)
        got_phase = got_phase + SLIP_GAIN * kicked
        incoming = shifted(radiation[:, -1:], "ta", 1)
        radiation = jnp.concatenate([incoming, radiation[:, :-1]], axis=1)
    filled = arrived_weight > 0
    result = jnp.stack([jnp.where(filled, got_phase, 0.0), jnp.where(filled, kicked, 0.0)])
    return (result, radiation)


def solution(mesh):
    return jax.shard_map(
        body,
        mesh=mesh,
        in_specs=(
            P(None, ("ta", "pb")),
            P(("ta", "pb")),
            P(("ta", "pb")),
            P(("ta", "pb"), None),
            P(("ta", "pb")),
            P(),
            P(),
            P(),
            P(),
            P(),
            P(),
        ),
        out_specs=(P(None, ("ta", "pb")), P(None, "ta")),
        check_vma=False,
    )
```

profile of v0, /device:TPU:32, one launch (start us, length us, event | category | flops | bytes accessed | tf_op | source)
XLA Modules:
  0.0 320.8 jit_solution(3291533808186617567)
XLA Ops:
  7.8 1.4 reduce.17
  9.3 4.0 %while.26 = (s32[]{:T(128)}, f32[32]{0:T(128)S(1)}, f32[8,512]{1,0:T(8,128)S(1)}, bf16[8,512,32]{1,2,0:T(8,128)(2,1)S(1)}, s32[]{:T(128)}, /*index=5*/s32[]{:T(128)}) while((s32[]{:T(128)}, f32[32]{0:T(128)S(1)}, f32[8,512]{1,0:T(8,128)S(1)}, bf16[8,512,32]{1,2,0:T(8,128)(2,1)S(1)}, s32[]{:T(128)}, /*index=5*/s32[]{:T(128)}) %tuple.81), condition=%wide.region_3.4_spmd.clone, body=%wide.region_0.3_spmd.clone.sunk | while | flops 17399332 | bytes 106719 | solution.py:60
  13.7 16.1 %scatter_custom_fusion.1 = s32[8192]{0:T(1024)} fusion(s32[4096]{0:T(1024)S(1)} %broadcast_select_fusion.2, s32[4096]{0:T(1024)S(1)} %get-tuple-element.186, s32[]{:T(128)} %constant.147.clone.1), kind=kCustom, calls=%fused_computation.109 | custom fusion | bytes 32772
  29.8 9.8 %all-to-all-start.1 = ((s32[1,32,256]{2,0,1:T(1,128)}), s32[1,32,256]{2,0,1:T(1,128)S(1)}, u32[]{:S(2)}, u32[]{:S(2)}) async-start(s32[1,32,256]{2,0,1:T(1,128)} %bitcast.8), calls=%async_computation.1 | async-start | bytes 65536 | tf_op jit(solution)/shard_map/all_to_all | solution.py:150
  41.4 12.8 %scatter_custom_fusion = f32[3,8192]{0,1:T(8,128)} fusion(s32[4096]{0:T(1024)S(1)} %bitcast.101, f32[4096,3]{1,0:T(8,128)S(1)} %copy.23, f32[]{:T(128)} %constant.145.clone.1), kind=kCustom, calls=%fused_computation.31 | custom fusion | bytes 98308 | tf_op jit(solution)/shard_map/scatter | solution.py:139
  54.2 3.5 %copy.24 = f32[3,32,256]{2,0,1:T(4,128)} copy(f32[3,32,256]{0,2,1:T(8,128)} %bitcast.82) | data formatting | bytes 196608 | tf_op jit(solution)/shard_map/reshape | solution.py:148
  57.9 9.8 %all-to-all-start = ((f32[3,32,256]{2,0,1:T(4,128)}), f32[3,32,256]{2,0,1:T(4,128)S(1)}, u32[]{:S(2)}, u32[]{:S(2)}) async-start(f32[3,32,256]{2,0,1:T(4,128)} %copy.24), calls=%async_computation | async-start | bytes 262144 | tf_op jit(solution)/shard_map/all_to_all | solution.py:147
  69.4 4.2 %all-to-all-done = f32[3,32,256]{2,0,1:T(4,128)S(1)} async-done(((f32[3,32,256]{2,0,1:T(4,128)}), f32[3,32,256]{2,0,1:T(4,128)S(1)}, u32[]{:S(2)}, u32[]{:S(2)}) %all-to-all-start) | async-done | bytes 98336 | tf_op jit(solution)/shard_map/all_to_all | solution.py:147
  74.2 30.3 %psum.22 = f32[2,4]{1,0:T(2,128)S(1)} all-reduce(f32[2,4]{1,0:T(2,128)S(1)} %pad_maximum_fusion.3), channel_id=1, replica_groups=mesh['ta'=32,'pb'=16] {'pb'}, use_global_device_ids=true, to_apply=%region_15.16 | all-reduce | flops 8 | bytes 64 | tf_op jit(solution)/shard_map/psum | solution.py:187
  104.6 8.0 %while.27 = (s32[]{:T(128)}, f32[384,96]{0,1:T(8,128)S(1)}, s32[4,2048]{1,0:T(4,128)S(1)}, s32[4,2048]{1,0:T(4,128)S(1)}, bf16[4,2048]{1,0:T(4,128)(2,1)S(1)}, /*index=5*/s32[]{:T(128)}, s32[]{:T(128)}) while((s32[]{:T(128)}, f32[384,96]{0,1:T(8,128)S(1)}, s32[4,2048]{1,0:T(4,128)S(1)}, s32[4,2048]{1,0:T(4,128)S(1)}, ...), condition=%wide.region_9.10_spmd.clone, body=%wide.region_8.9_spmd.clone.sunk | while | flops 153069568 | bytes 5517415 | solution.py:89
  105.6 1.0 convolution_add_fusion.3
  109.6 1.0 convolution_add_fusion.3
  113.7 2.5 collective-permute-start.2
  116.2 101.6 %all-reduce.6.cloned.1.call-done = f32[4,9216]{1,0:T(4,128)} async-done(((f32[4,9216]{1,0:T(4,128)}), f32[4,9216]{1,0:T(4,128)}) %all-reduce.6.cloned.1.call-update) | async-done | bytes 147472 | tf_op jit(solution)/shard_map/psum | solution.py:164
  217.9 1.0 fusion.37
  218.9 3.4 %collective-permute-start.1 = (f32[1,9216]{1,0:T(1,128)S(1)}, f32[1,9216]{1,0:T(1,128)S(1)}, u32[]{:S(2)}, u32[]{:S(2)}) collective-permute-start(f32[1,9216]{1,0:T(1,128)S(1)} %get-tuple-element.177), channel_id=1, source_target_pairs={{0,16},{16,32},{32,48},{48,64},{64,80},{80,96},{96,112},{112,128},... | collective-permute-start | bytes 110600 | tf_op jit(solution)/shard_map/ppermute | solution.py:24
  222.3 6.0 %collective-permute-start = (f32[1,9216]{1,0:T(1,128)S(1)}, f32[1,9216]{1,0:T(1,128)S(1)}, u32[]{:S(2)}, u32[]{:S(2)}) collective-permute-start(f32[1,9216]{1,0:T(1,128)S(1)} %get-tuple-element.176), channel_id=1, source_target_pairs={{16,0},{32,16},{48,32},{64,48},{80,64},{96,80},{112,96},{128,112},... | collective-permute-start | bytes 110600 | tf_op jit(solution)/shard_map/ppermute | solution.py:25
  228.5 1.2 collective-permute-done
  229.7 2.0 fusion.19
  231.8 45.5 %gather_fusion = f32[8192]{0:T(1024)S(1)} fusion(f32[36864]{0:T(1024)S(1)} %bitcast.81, s32[8192]{0:T(1024)S(1)} %broadcast_clamp_fusion), kind=kCustom, calls=%fused_computation | custom fusion | bytes 98304 | tf_op jit(solution)/shard_map/jit(_take)/gather | solution.py:168
  278.0 23.5 %psum.23 = f32[2,4]{1,0:T(2,128)S(1)} all-reduce(f32[2,4]{1,0:T(2,128)S(1)} %pad_maximum_fusion.4), channel_id=1, replica_groups=mesh['ta'=32,'pb'=16] {'pb'}, use_global_device_ids=true, to_apply=%region_20.21 | all-reduce | flops 8 | bytes 64 | tf_op jit(solution)/shard_map/psum | solution.py:187
  301.9 2.2 add_select_fusion.8
  304.3 1.9 collective-permute-start.3
  306.9 6.5 %collective-permute-done.3 = f32[2,1]{1,0:T(2,128)S(1)} collective-permute-done((f32[2,1]{1,0:T(2,128)S(1)}, f32[2,1]{1,0:T(2,128)S(1)}, u32[]{:S(2)}, u32[]{:S(2)}) %collective-permute-start.3) | collective-permute-done | bytes 40 | tf_op jit(solution)/shard_map/ppermute | solution.py:33
  (151 shorter events, 18.4 us)
Async XLA Ops:
  7.2 6.2 %copy-start.12 = (s32[2]{0:T(128)S(1)}, s32[2]{0:T(128)}, u32[]{:S(2)}) copy-start(s32[2]{0:T(128)} %constant.174) | copy-start | bytes 28
  7.2 6.3 %copy-start.11 = (s32[2]{0:T(128)S(1)}, s32[2]{0:T(128)}, u32[]{:S(2)}) copy-start(s32[2]{0:T(128)} %constant.171) | copy-start | bytes 28
  7.2 6.1 %copy-start = (s32[4096,1]{0,1:T(1,128)S(1)}, s32[4096,1]{0,1:T(1,128)}, u32[]{:S(2)}) copy-start(s32[4096,1]{0,1:T(1,128)} %param.18) | copy-start | bytes 49156
  7.2 6.4 %copy-start.4 = (s32[4096]{0:T(1024)S(1)}, s32[4096]{0:T(1024)}, u32[]{:S(2)}) copy-start(s32[4096]{0:T(1024)} %param.17) | copy-start | bytes 49156
  7.2 6.4 %copy-start.5 = (s32[4096]{0:T(1024)S(1)}, s32[4096]{0:T(1024)}, u32[]{:S(2)}) copy-start(s32[4096]{0:T(1024)} %param.19) | copy-start | bytes 49156
  7.2 32.4 %copy-start.6 = (bf16[4096]{0:T(1024)(128)(2,1)S(1)}, bf16[4096]{0:T(1024)(128)(2,1)}, u32[]{:S(2)}) copy-start(bf16[4096]{0:T(1024)(128)(2,1)} %param.16) | copy-start | bytes 24580
  7.2 32.4 %copy-start.7 = (f32[96]{0:T(128)S(1)}, f32[96]{0:T(128)}, u32[]{:S(2)}) copy-start(f32[96]{0:T(128)} %param.21) | copy-start | bytes 1156
  7.2 32.4 %copy-start.8 = (f32[96]{0:T(128)S(1)}, f32[96]{0:T(128)}, u32[]{:S(2)}) copy-start(f32[96]{0:T(128)} %param.20) | copy-start | bytes 1156
  7.3 33.0 %copy-start.3 = (f32[2,4096]{1,0:T(2,128)S(1)}, f32[2,4096]{1,0:T(2,128)}, u32[]{:S(2)}) copy-start(f32[2,4096]{1,0:T(2,128)} %param.15) | copy-start | bytes 98308
  29.8 28.1 %all-to-all-start.1 = ((s32[1,32,256]{2,0,1:T(1,128)}), s32[1,32,256]{2,0,1:T(1,128)S(1)}, u32[]{:S(2)}, u32[]{:S(2)}) async-start(s32[1,32,256]{2,0,1:T(1,128)} %bitcast.8), calls=%async_computation.1 | async-start | bytes 65536 | tf_op jit(solution)/shard_map/all_to_all | solution.py:150
  54.2 3.5 %copy-start.1 = (f32[96,96]{1,0:T(8,128)S(1)}, f32[96,96]{1,0:T(8,128)}, u32[]{:S(2)}) copy-start(f32[96,96]{1,0:T(8,128)} %param.25) | copy-start | bytes 110596
  54.2 3.6 %copy-start.2 = (f32[96,96]{1,0:T(8,128)S(1)}, f32[96,96]{1,0:T(8,128)}, u32[]{:S(2)}) copy-start(f32[96,96]{1,0:T(8,128)} %param.24) | copy-start | bytes 110596
  54.2 14.2 %copy-start.9 = (f32[96]{0:T(128)S(1)}, f32[96]{0:T(128)}, u32[]{:S(2)}) copy-start(f32[96]{0:T(128)} %param.23) | copy-start | bytes 1156
  54.2 14.2 %copy-start.10 = (f32[96]{0:T(128)S(1)}, f32[96]{0:T(128)}, u32[]{:S(2)}) copy-start(f32[96]{0:T(128)} %param.22) | copy-start | bytes 1156
  57.9 15.7 %all-to-all-start = ((f32[3,32,256]{2,0,1:T(4,128)}), f32[3,32,256]{2,0,1:T(4,128)S(1)}, u32[]{:S(2)}, u32[]{:S(2)}) async-start(f32[3,32,256]{2,0,1:T(4,128)} %copy.24), calls=%async_computation | async-start | bytes 262144 | tf_op jit(solution)/shard_map/all_to_all | solution.py:147
  67.7 150.2 %all-reduce.6.cloned.1.call-start = ((), (), s32[]{:S(2)}) async-start(), calls=%async_computation.2 | async-start | bytes 294912 | tf_op jit(solution)/shard_map/psum | solution.py:164
  113.7 187.8 %collective-permute-start.2 = (f32[2,1]{1,0:T(2,128)S(1)}, f32[2,1]{1,0:T(2,128)S(1)}, u32[]{:S(2)}, u32[]{:S(2)}) collective-permute-start(f32[2,1]{1,0:T(2,128)S(1)} %slice.85), channel_id=1, source_target_pairs={{0,16},{16,32},{32,48},{48,64},{64,80},{80,96},{96,112},{112,128},... | collective-permute-start | bytes 32 | tf_op jit(solution)/shard_map/ppermute | solution.py:33
  218.9 9.6 %collective-permute-start.1 = (f32[1,9216]{1,0:T(1,128)S(1)}, f32[1,9216]{1,0:T(1,128)S(1)}, u32[]{:S(2)}, u32[]{:S(2)}) collective-permute-start(f32[1,9216]{1,0:T(1,128)S(1)} %get-tuple-element.177), channel_id=1, source_target_pairs={{0,16},{16,32},{32,48},{48,64},{64,80},{80,96},{96,112},{112,128},... | collective-permute-start | bytes 110600 | tf_op jit(solution)/shard_map/ppermute | solution.py:24
  222.3 7.4 %collective-permute-start = (f32[1,9216]{1,0:T(1,128)S(1)}, f32[1,9216]{1,0:T(1,128)S(1)}, u32[]{:S(2)}, u32[]{:S(2)}) collective-permute-start(f32[1,9216]{1,0:T(1,128)S(1)} %get-tuple-element.176), channel_id=1, source_target_pairs={{16,0},{32,16},{48,32},{64,48},{80,64},{96,80},{112,96},{128,112},... | collective-permute-start | bytes 110600 | tf_op jit(solution)/shard_map/ppermute | solution.py:25
  304.3 9.1 %collective-permute-start.3 = (f32[2,1]{1,0:T(2,128)S(1)}, f32[2,1]{1,0:T(2,128)S(1)}, u32[]{:S(2)}, u32[]{:S(2)}) collective-permute-start(f32[2,1]{1,0:T(2,128)S(1)} %slice.89), channel_id=1, source_target_pairs={{0,16},{16,32},{32,48},{48,64},{64,80},{80,96},{96,112},{112,128},... | collective-permute-start | bytes 32 | tf_op jit(solution)/shard_map/ppermute | solution.py:33
Sparse Core Ops, SparseCore 0:
  113.8 104.0 all-reduce.5
where the time goes:
time: 321 us
  waiting for transfers between devices  114 us (36%)
  local copies, waits for them, and re-layouts  82.4 us (26%)
  blocking collectives  53.8 us (17%)
  starting transfers between devices  33.4 us (10%)
  other arithmetic  16.3 us (5%)
  between operations  14.6 us (5%)
  matrix products  6.37 us (2%)
    psum x1, waiting for transfers between devices, body(): summed = lax.psum(partial_value, 'pb')  102 us
    psum x2, blocking collectives, body(): bunching = lax.psum(local_sums, 'pb')  53.8 us
    gather x1, local copies, waits for them, and re-layouts, body(): kicked = got_float[1] + jnp.take(force_map.reshape(-1), combined)  45.5 us
    unnamed x30, local copies, waits for them, and re-layouts  16.7 us
    scatter x1, local copies, waits for them, and re-layouts, body(): send_float = jnp.zeros((3, slot_count), jnp.float32).at[:, position].set(...  12.8 us
    all_to_all x1, starting transfers between devices, body(): lax.all_to_all(send_index.reshape(1, groups, capacity), 'ta', split_axis=...  9.83 us
    all_to_all x1, starting transfers between devices, body(): lax.all_to_all(send_float.reshape(3, groups, capacity), 'ta', split_axis=...  9.79 us
    ppermute x2, waiting for transfers between devices, shifted(): lax.ppermute(value, axis, [(source, source + steps) for source in range(l...  6.48 us
  transfers between devices with their start and end apart: 7, of which 4 were waited for; matrix products, arithmetic and copies ran while one was open for 22% of the time, Pallas kernels for 0%

commit v1 on v0

--- a/solution.py
+++ b/solution.py
@@ -184,7 +184,7 @@
                 jnp.sum(select * (-weighted * sine_part)[None, :], axis=1),
             ]
         )
-        bunching = lax.psum(local_sums, "pb")
+        bunching = jnp.sum(lax.all_gather(local_sums, "pb"), axis=0)
         radiation = radiation + couple * bunching
         real_here = jnp.sum(select * radiation[0][:, None], axis=0)
         imag_here = jnp.sum(select * radiation[1][:, None], axis=0)

time: 321 us -> 305 us (0.950)
  blocking collectives: 53.8 us -> 38 us
    psum x2 -> x0, blocking collectives: 53.8 us -> none  [body(): bunching = lax.psum(local_sums, 'pb')]
    all_gather x0 -> x2, blocking collectives: none -> 38 us  [body(): bunching = jnp.sum(lax.all_gather(local_sums, 'pb'), axis=0)]
  transfers between devices with their start and end apart: 7 -> 7, of which waited for: 4 -> 4; matrix products, arithmetic and copies ran while one was open for 22% -> 23% of each run, Pallas kernels for 0% -> 0%
where the time goes in v1:
time: 305 us; the launch traced here: 304 us
  waiting for transfers between devices  113 us (37%)
  local copies, waits for them, and re-layouts  82.4 us (27%)
  blocking collectives  38 us (12%)
  starting transfers between devices  33.4 us (11%)
  other arithmetic  16.3 us (5%)
  between operations  14.6 us (5%)
  matrix products  6.37 us (2%)
    psum x1, waiting for transfers between devices, body(): summed = lax.psum(partial_value, 'pb')  101 us
    gather x1, local copies, waits for them, and re-layouts, body(): kicked = got_float[1] + jnp.take(force_map.reshape(-1), combined)  45.5 us
    all_gather x2, blocking collectives, body(): bunching = jnp.sum(lax.all_gather(local_sums, 'pb'), axis=0)  38 us
    unnamed x30, local copies, waits for them, and re-layouts  16.7 us
    scatter x1, local copies, waits for them, and re-layouts, body(): send_float = jnp.zeros((3, slot_count), jnp.float32).at[:, position].set(...  12.8 us
    all_to_all x1, starting transfers between devices, body(): lax.all_to_all(send_index.reshape(1, groups, capacity), 'ta', split_axis=...  9.83 us
    all_to_all x1, starting transfers between devices, body(): lax.all_to_all(send_float.reshape(3, groups, capacity), 'ta', split_axis=...  9.79 us
    ppermute x2, waiting for transfers between devices, shifted(): lax.ppermute(value, axis, [(source, source + steps) for source in range(l...  6.48 us
  transfers between devices with their start and end apart: 7, of which 4 were waited for; matrix products, arithmetic and copies ran while one was open for 23% of the time, Pallas kernels for 0%

profile of v1, /device:TPU:32, one launch (start us, length us, event | category | flops | bytes accessed | tf_op | source)
XLA Modules:
  0.0 304.2 jit_solution(13047001155948594587)
XLA Ops:
  7.8 1.4 reduce.19
  9.3 4.0 %while.26 = (s32[]{:T(128)}, f32[32]{0:T(128)S(1)}, f32[8,512]{1,0:T(8,128)S(1)}, bf16[8,512,32]{1,2,0:T(8,128)(2,1)S(1)}, s32[]{:T(128)}, /*index=5*/s32[]{:T(128)}) while((s32[]{:T(128)}, f32[32]{0:T(128)S(1)}, f32[8,512]{1,0:T(8,128)S(1)}, bf16[8,512,32]{1,2,0:T(8,128)(2,1)S(1)}, s32[]{:T(128)}, /*index=5*/s32[]{:T(128)}) %tuple.81), condition=%wide.region_3.4_spmd.clone, body=%wide.region_0.3_spmd.clone.sunk | while | flops 17399332 | bytes 106719 | solution.py:60
  13.7 16.1 %scatter_custom_fusion.1 = s32[8192]{0:T(1024)} fusion(s32[4096]{0:T(1024)S(1)} %broadcast_select_fusion.2, s32[4096]{0:T(1024)S(1)} %get-tuple-element.186, s32[]{:T(128)} %constant.147.clone.1), kind=kCustom, calls=%fused_computation.109 | custom fusion | bytes 32772
  29.8 9.8 %all-to-all-start.1 = ((s32[1,32,256]{2,0,1:T(1,128)}), s32[1,32,256]{2,0,1:T(1,128)S(1)}, u32[]{:S(2)}, u32[]{:S(2)}) async-start(s32[1,32,256]{2,0,1:T(1,128)} %bitcast.8), calls=%async_computation.1 | async-start | bytes 65536 | tf_op jit(solution)/shard_map/all_to_all | solution.py:150
  41.4 12.8 %scatter_custom_fusion = f32[3,8192]{0,1:T(8,128)} fusion(s32[4096]{0:T(1024)S(1)} %bitcast.105, f32[4096,3]{1,0:T(8,128)S(1)} %copy.23, f32[]{:T(128)} %constant.145.clone.1), kind=kCustom, calls=%fused_computation.31 | custom fusion | bytes 98308 | tf_op jit(solution)/shard_map/scatter | solution.py:139
  54.2 3.5 %copy.24 = f32[3,32,256]{2,0,1:T(4,128)} copy(f32[3,32,256]{0,2,1:T(8,128)} %bitcast.86) | data formatting | bytes 196608 | tf_op jit(solution)/shard_map/reshape | solution.py:148
  57.9 9.8 %all-to-all-start = ((f32[3,32,256]{2,0,1:T(4,128)}), f32[3,32,256]{2,0,1:T(4,128)S(1)}, u32[]{:S(2)}, u32[]{:S(2)}) async-start(f32[3,32,256]{2,0,1:T(4,128)} %copy.24), calls=%async_computation | async-start | bytes 262144 | tf_op jit(solution)/shard_map/all_to_all | solution.py:147
  69.4 4.2 %all-to-all-done = f32[3,32,256]{2,0,1:T(4,128)S(1)} async-done(((f32[3,32,256]{2,0,1:T(4,128)}), f32[3,32,256]{2,0,1:T(4,128)S(1)}, u32[]{:S(2)}, u32[]{:S(2)}) %all-to-all-start) | async-done | bytes 98336 | tf_op jit(solution)/shard_map/all_to_all | solution.py:147
  74.2 23.2 %all-gather.2 = f32[16,2,4]{2,1,0:T(2,128)S(1)} all-gather(f32[1,2,4]{2,1,0:T(2,128)S(1)} %maximum_bitcast_fusion.1), channel_id=2, replica_groups=mesh['ta'=32,'pb'=16] {'pb'}, dimensions={0}, use_global_device_ids=true | all-gather | bytes 544 | tf_op jit(solution)/shard_map/all_gather | solution.py:187
  97.6 8.0 %while.27 = (s32[]{:T(128)}, f32[384,96]{0,1:T(8,128)S(1)}, s32[4,2048]{1,0:T(4,128)S(1)}, s32[4,2048]{1,0:T(4,128)S(1)}, bf16[4,2048]{1,0:T(4,128)(2,1)S(1)}, /*index=5*/s32[]{:T(128)}, s32[]{:T(128)}) while((s32[]{:T(128)}, f32[384,96]{0,1:T(8,128)S(1)}, s32[4,2048]{1,0:T(4,128)S(1)}, s32[4,2048]{1,0:T(4,128)S(1)}, ...), condition=%wide.region_9.10_spmd.clone, body=%wide.region_8.9_spmd.clone.sunk | while | flops 153069568 | bytes 5517415 | solution.py:89
  100.5 1.0 convolution_add_fusion.3
  102.5 1.0 convolution_add_fusion.3
  106.7 2.5 collective-permute-start.2
  109.2 100.7 %all-reduce.6.cloned.1.call-done = f32[4,9216]{1,0:T(4,128)} async-done(((f32[4,9216]{1,0:T(4,128)}), f32[4,9216]{1,0:T(4,128)}) %all-reduce.6.cloned.1.call-update) | async-done | bytes 147472 | tf_op jit(solution)/shard_map/psum | solution.py:164
  209.9 1.0 fusion.37
  211.0 3.4 %collective-permute-start.1 = (f32[1,9216]{1,0:T(1,128)S(1)}, f32[1,9216]{1,0:T(1,128)S(1)}, u32[]{:S(2)}, u32[]{:S(2)}) collective-permute-start(f32[1,9216]{1,0:T(1,128)S(1)} %get-tuple-element.177), channel_id=1, source_target_pairs={{0,16},{16,32},{32,48},{48,64},{64,80},{80,96},{96,112},{112,128},... | collective-permute-start | bytes 110600 | tf_op jit(solution)/shard_map/ppermute | solution.py:24
  214.4 6.0 %collective-permute-start = (f32[1,9216]{1,0:T(1,128)S(1)}, f32[1,9216]{1,0:T(1,128)S(1)}, u32[]{:S(2)}, u32[]{:S(2)}) collective-permute-start(f32[1,9216]{1,0:T(1,128)S(1)} %get-tuple-element.176), channel_id=1, source_target_pairs={{16,0},{32,16},{48,32},{64,48},{80,64},{96,80},{112,96},{128,112},... | collective-permute-start | bytes 110600 | tf_op jit(solution)/shard_map/ppermute | solution.py:25
  220.6 1.2 collective-permute-done
  221.8 2.0 fusion.19
  223.8 45.5 %gather_fusion = f32[8192]{0:T(1024)S(1)} fusion(f32[36864]{0:T(1024)S(1)} %bitcast.85, s32[8192]{0:T(1024)S(1)} %broadcast_clamp_fusion), kind=kCustom, calls=%fused_computation | custom fusion | bytes 98304 | tf_op jit(solution)/shard_map/jit(_take)/gather | solution.py:168
  270.0 14.8 %all-gather.3 = f32[16,2,4]{2,1,0:T(2,128)S(1)} all-gather(f32[1,2,4]{2,1,0:T(2,128)S(1)} %maximum_bitcast_fusion.2), channel_id=3, replica_groups=mesh['ta'=32,'pb'=16] {'pb'}, dimensions={0}, use_global_device_ids=true | all-gather | bytes 544 | tf_op jit(solution)/shard_map/all_gather | solution.py:187
  285.3 2.2 add_select_fusion.8
  287.6 1.9 collective-permute-start.3
  290.2 6.5 %collective-permute-done.3 = f32[2,1]{1,0:T(2,128)S(1)} collective-permute-done((f32[2,1]{1,0:T(2,128)S(1)}, f32[2,1]{1,0:T(2,128)S(1)}, u32[]{:S(2)}, u32[]{:S(2)}) %collective-permute-start.3) | collective-permute-done | bytes 40 | tf_op jit(solution)/shard_map/ppermute | solution.py:33
  (153 shorter events, 18.4 us)
Async XLA Ops:
  7.2 6.2 %copy-start.12 = (s32[2]{0:T(128)S(1)}, s32[2]{0:T(128)}, u32[]{:S(2)}) copy-start(s32[2]{0:T(128)} %constant.174) | copy-start | bytes 28
  7.2 6.3 %copy-start.11 = (s32[2]{0:T(128)S(1)}, s32[2]{0:T(128)}, u32[]{:S(2)}) copy-start(s32[2]{0:T(128)} %constant.171) | copy-start | bytes 28
  7.2 6.1 %copy-start = (s32[4096,1]{0,1:T(1,128)S(1)}, s32[4096,1]{0,1:T(1,128)}, u32[]{:S(2)}) copy-start(s32[4096,1]{0,1:T(1,128)} %param.18) | copy-start | bytes 49156
  7.2 6.4 %copy-start.4 = (s32[4096]{0:T(1024)S(1)}, s32[4096]{0:T(1024)}, u32[]{:S(2)}) copy-start(s32[4096]{0:T(1024)} %param.17) | copy-start | bytes 49156
  7.2 6.4 %copy-start.5 = (s32[4096]{0:T(1024)S(1)}, s32[4096]{0:T(1024)}, u32[]{:S(2)}) copy-start(s32[4096]{0:T(1024)} %param.19) | copy-start | bytes 49156
  7.2 32.4 %copy-start.6 = (bf16[4096]{0:T(1024)(128)(2,1)S(1)}, bf16[4096]{0:T(1024)(128)(2,1)}, u32[]{:S(2)}) copy-start(bf16[4096]{0:T(1024)(128)(2,1)} %param.16) | copy-start | bytes 24580
  7.2 32.4 %copy-start.7 = (f32[96]{0:T(128)S(1)}, f32[96]{0:T(128)}, u32[]{:S(2)}) copy-start(f32[96]{0:T(128)} %param.21) | copy-start | bytes 1156
  7.2 32.4 %copy-start.8 = (f32[96]{0:T(128)S(1)}, f32[96]{0:T(128)}, u32[]{:S(2)}) copy-start(f32[96]{0:T(128)} %param.20) | copy-start | bytes 1156
  7.3 33.0 %copy-start.3 = (f32[2,4096]{1,0:T(2,128)S(1)}, f32[2,4096]{1,0:T(2,128)}, u32[]{:S(2)}) copy-start(f32[2,4096]{1,0:T(2,128)} %param.15) | copy-start | bytes 98308
  29.8 28.1 %all-to-all-start.1 = ((s32[1,32,256]{2,0,1:T(1,128)}), s32[1,32,256]{2,0,1:T(1,128)S(1)}, u32[]{:S(2)}, u32[]{:S(2)}) async-start(s32[1,32,256]{2,0,1:T(1,128)} %bitcast.8), calls=%async_computation.1 | async-start | bytes 65536 | tf_op jit(solution)/shard_map/all_to_all | solution.py:150
  54.2 3.5 %copy-start.1 = (f32[96,96]{1,0:T(8,128)S(1)}, f32[96,96]{1,0:T(8,128)}, u32[]{:S(2)}) copy-start(f32[96,96]{1,0:T(8,128)} %param.25) | copy-start | bytes 110596
  54.2 3.6 %copy-start.2 = (f32[96,96]{1,0:T(8,128)S(1)}, f32[96,96]{1,0:T(8,128)}, u32[]{:S(2)}) copy-start(f32[96,96]{1,0:T(8,128)} %param.24) | copy-start | bytes 110596
  54.2 14.2 %copy-start.9 = (f32[96]{0:T(128)S(1)}, f32[96]{0:T(128)}, u32[]{:S(2)}) copy-start(f32[96]{0:T(128)} %param.23) | copy-start | bytes 1156
  54.2 14.2 %copy-start.10 = (f32[96]{0:T(128)S(1)}, f32[96]{0:T(128)}, u32[]{:S(2)}) copy-start(f32[96]{0:T(128)} %param.22) | copy-start | bytes 1156
  57.9 15.7 %all-to-all-start = ((f32[3,32,256]{2,0,1:T(4,128)}), f32[3,32,256]{2,0,1:T(4,128)S(1)}, u32[]{:S(2)}, u32[]{:S(2)}) async-start(f32[3,32,256]{2,0,1:T(4,128)} %copy.24), calls=%async_computation | async-start | bytes 262144 | tf_op jit(solution)/shard_map/all_to_all | solution.py:147
  67.7 142.2 %all-reduce.6.cloned.1.call-start = ((), (), s32[]{:S(2)}) async-start(), calls=%async_computation.2 | async-start | bytes 294912 | tf_op jit(solution)/shard_map/psum | solution.py:164
  106.7 178.2 %collective-permute-start.2 = (f32[2,1]{1,0:T(2,128)S(1)}, f32[2,1]{1,0:T(2,128)S(1)}, u32[]{:S(2)}, u32[]{:S(2)}) collective-permute-start(f32[2,1]{1,0:T(2,128)S(1)} %slice.85), channel_id=1, source_target_pairs={{0,16},{16,32},{32,48},{48,64},{64,80},{80,96},{96,112},{112,128},... | collective-permute-start | bytes 32 | tf_op jit(solution)/shard_map/ppermute | solution.py:33
  211.0 9.6 %collective-permute-start.1 = (f32[1,9216]{1,0:T(1,128)S(1)}, f32[1,9216]{1,0:T(1,128)S(1)}, u32[]{:S(2)}, u32[]{:S(2)}) collective-permute-start(f32[1,9216]{1,0:T(1,128)S(1)} %get-tuple-element.177), channel_id=1, source_target_pairs={{0,16},{16,32},{32,48},{48,64},{64,80},{80,96},{96,112},{112,128},... | collective-permute-start | bytes 110600 | tf_op jit(solution)/shard_map/ppermute | solution.py:24
  214.4 7.4 %collective-permute-start = (f32[1,9216]{1,0:T(1,128)S(1)}, f32[1,9216]{1,0:T(1,128)S(1)}, u32[]{:S(2)}, u32[]{:S(2)}) collective-permute-start(f32[1,9216]{1,0:T(1,128)S(1)} %get-tuple-element.176), channel_id=1, source_target_pairs={{16,0},{32,16},{48,32},{64,48},{80,64},{96,80},{112,96},{128,112},... | collective-permute-start | bytes 110600 | tf_op jit(solution)/shard_map/ppermute | solution.py:25
  287.6 9.1 %collective-permute-start.3 = (f32[2,1]{1,0:T(2,128)S(1)}, f32[2,1]{1,0:T(2,128)S(1)}, u32[]{:S(2)}, u32[]{:S(2)}) collective-permute-start(f32[2,1]{1,0:T(2,128)S(1)} %slice.89), channel_id=1, source_target_pairs={{0,16},{16,32},{32,48},{48,64},{64,80},{80,96},{96,112},{112,128},... | collective-permute-start | bytes 32 | tf_op jit(solution)/shard_map/ppermute | solution.py:33
Sparse Core Ops, SparseCore 0:
  106.7 103.1 all-reduce.5
